TPU v7x, 32 devices: a whole 2x2x4 slice. The times are simulated.
32 devices in a mesh: ctx: 4 (over y, core), row: 8 (over z, x).
Axes of the slice: x: 2, y: 2, z: 4, core: 2. Of those that a mesh axis runs over, the one named last changes fastest.
Arguments:
- queries: bfloat16 [16, 2, 4096], P('row'), may hold values from -400 to 400
- prefix_id: int32 [16], P('row'), may hold values from 0 to 7
- prefix_keys: bfloat16 [8, 1024, 512], P(None, ('ctx', 'row')), may hold values from -8 to 8
- prefix_values: bfloat16 [8, 1024, 512], P(None, ('ctx', 'row')), may hold values from -6 to 6
- pool_keys: bfloat16 [512, 64, 512], P(('ctx', 'row')), may hold values from -5 to 5
- pool_values: bfloat16 [512, 64, 512], P(('ctx', 'row')), may hold values from -6 to 6
- page_table: int32 [16, 32], P('row'), may hold values from 0 to 511, as said below
- suffix_len: int32 [16], P('row'), may hold values from 256 to 2048
- new_keys: bfloat16 [16, 2, 512], P('row'), may hold values from -6.25 to 6.25
- new_values: bfloat16 [16, 2, 512], P('row'), may hold values from -6 to 6
Outputs:
- attended: bfloat16 [16, 2, 4096], P('row')
Inputs may be any that keep to these rules, and one draw needn't show every extreme that they name: `page_table`: the 64 entries of the rows i with one value of i // 2 name different pool pages p with (p // 16) % (8) == i // 2, and together they name all such pages.
All inputs are finite; a program needn't handle non-finite values.
Results may differ from a plain program's by a relative error of at most 0.003.
Values may be sent and summed in bfloat16 or wider, within the bound.
No kernel may reach another device: no remote copies, remote signals or barrier semaphores. Data moves between devices by JAX's collectives and lax.ppermute only.
A program may use at most 64 MiB of HBM per device.

v0:
```python
import math
import jax
import jax.numpy as jnp
from jax import lax
from jax.sharding import PartitionSpec as P

H = 32
KVH = 4
HD = 128
MASKED_SCORE = -1e30


def joined(value, axis, join):
    pieces = jax.tree.map(lambda part: lax.all_gather(part, axis), value)
    head = jax.tree.map(lambda part: part[0], pieces)
    tail = jax.tree.map(lambda part: part[1:], pieces)
    running, _ = lax.scan(lambda running, share: (join(running, share), None), head, tail)
    return running


def combine_pair(earlier, later):
    highest = jnp.maximum(earlier[0], later[0])
    left_factor = jnp.exp(earlier[0] - highest)
    right_factor = jnp.exp(later[0] - highest)
    totals = left_factor * earlier[1] + right_factor * later[1]
    sums = left_factor[..., None] * earlier[2] + right_factor[..., None] * later[2]
    return (highest, totals, sums)


def fold_stack(stacked):
    peak_stack, total_stack, sum_stack = stacked
    highest = jnp.max(peak_stack, axis=0)
    factor = jnp.exp(peak_stack - highest[None])
    return (
        highest,
        jnp.sum(factor * total_stack, axis=0),
        jnp.sum(factor[..., None] * sum_stack, axis=0),
    )


def block_stats(scores, valid_mask, values, einsum_form):
    block_peak = jnp.max(jnp.where(valid_mask, scores, MASKED_SCORE), axis=-1)
    weights = jnp.where(valid_mask, jnp.exp(scores - block_peak[..., None]), 0.0).astype(
        jnp.bfloat16
    )
    block_total = jnp.sum(weights.astype(jnp.float32), axis=-1)
    block_sum = jnp.einsum(einsum_form, weights, values, preferred_element_type=jnp.float32)
    return (block_peak, block_total, block_sum)


def heads_merged(stats):
    lead = stats[0].shape[:2]
    return (
        stats[0].reshape(lead + (H,)),
        stats[1].reshape(lead + (H,)),
        stats[2].reshape(lead + (H, HD)),
    )


def per_device(
    queries,
    prefix_id,
    prefix_keys,
    prefix_values,
    pool_keys,
    pool_values,
    page_table,
    suffix_len,
    new_keys,
    new_values,
):
    rows_dev, step_count, feature_width = queries.shape
    groups = H // KVH
    score_scale = 1.0 / math.sqrt(HD)
    row_count = lax.axis_size("row")
    row_index = lax.axis_index("row")
    flat_index = lax.axis_index("ctx") * row_count + row_index
    own_query = queries.reshape(rows_dev, step_count, KVH, groups, HD)
    slot_count, page_len, kv_width = pool_keys.shape
    slot_ids = flat_index * slot_count + jnp.arange(slot_count, dtype=jnp.int32)
    slot_match = page_table[:, :, None] == slot_ids[None, None, :]
    entry_pos = jnp.arange(page_table.shape[1], dtype=jnp.int32)
    page_of = jnp.sum(jnp.where(slot_match, entry_pos[None, :, None], 0), axis=1)
    owned = jnp.any(slot_match, axis=1)
    token_pos = (
        page_of[:, :, None] * page_len + jnp.arange(page_len, dtype=jnp.int32)[None, None, :]
    )
    live_mask = owned[:, :, None] & (token_pos < suffix_len[:, None, None])
    live_mask = live_mask.reshape(rows_dev, 1, 1, 1, slot_count * page_len)
    flat_keys = pool_keys.reshape(slot_count * page_len, KVH, HD)
    flat_values = pool_values.reshape(slot_count * page_len, KVH, HD)
    suffix_scores = (
        jnp.einsum("rskgd,tkd->rskgt", own_query, flat_keys, preferred_element_type=jnp.float32)
        * score_scale
    )
    suffix_stats = block_stats(suffix_scores, live_mask, flat_values, "rskgt,tkd->rskgd")
    fresh_keys = new_keys.reshape(rows_dev, step_count, KVH, HD)
    fresh_values = new_values.reshape(rows_dev, step_count, KVH, HD)
    fresh_scores = (
        jnp.einsum("rskgd,rtkd->rskgt", own_query, fresh_keys, preferred_element_type=jnp.float32)
        * score_scale
    )
    causal = jnp.arange(step_count)[None, :] <= jnp.arange(step_count)[:, None]
    causal = causal.reshape(1, step_count, 1, 1, step_count)
    fresh_stats = heads_merged(block_stats(fresh_scores, causal, fresh_values, "rskgt,rtkd->rskgd"))
    every_query, every_prefix = (
        lax.all_gather(queries, "row", axis=0, tiled=True),
        lax.all_gather(prefix_id, "row", axis=0, tiled=True),
    )
    total_rows = every_query.shape[0]
    span_len = prefix_keys.shape[1]
    row_keys = jnp.take(prefix_keys, every_prefix, axis=0).reshape(total_rows, span_len, KVH, HD)
    row_values = jnp.take(prefix_values, every_prefix, axis=0).reshape(
        total_rows, span_len, KVH, HD
    )
    every_row = every_query.reshape(total_rows, step_count, KVH, groups, HD)
    prefix_scores = (
        jnp.einsum("rskgd,rtkd->rskgt", every_row, row_keys, preferred_element_type=jnp.float32)
        * score_scale
    )
    always = jnp.ones((1, 1, 1, 1, span_len), dtype=bool)
    prefix_stats = block_stats(prefix_scores, always, row_values, "rskgt,rtkd->rskgd")
    row_start = row_index * rows_dev
    own_prefix = tuple(
        (lax.dynamic_slice_in_dim(member, row_start, rows_dev, 0) for member in prefix_stats)
    )
    own_merged = combine_pair(own_prefix, suffix_stats)
    whole_stats = tuple(
        (
            lax.dynamic_update_slice_in_dim(whole_arr, piece_arr, row_start, 0)
            for whole_arr, piece_arr in zip(prefix_stats, own_merged)
        )
    )
    block_peak, block_total, block_sum = heads_merged(whole_stats)
    stacked = (
        lax.all_to_all(block_peak[None], "row", split_axis=1, concat_axis=0, tiled=True),
        lax.all_to_all(block_total[None], "row", split_axis=1, concat_axis=0, tiled=True),
        lax.all_to_all(block_sum[None], "row", split_axis=1, concat_axis=0, tiled=True),
    )
    local_stats = fold_stack(stacked)
    merged = joined(local_stats, "ctx", combine_pair)
    final_stats = combine_pair(merged, fresh_stats)
    result = (final_stats[2] / final_stats[1][..., None]).astype(jnp.bfloat16)
    return result.reshape(rows_dev, step_count, H * HD)


def solution(mesh):
    in_specs = (
        P("row", None, None),
        P("row"),
        P(None, ("ctx", "row"), None),
        P(None, ("ctx", "row"), None),
        P(("ctx", "row"), None, None),
        P(("ctx", "row"), None, None),
        P("row", None),
        P("row"),
        P("row", None, None),
        P("row", None, None),
    )
    out_specs = P("row", None, None)
    return jax.shard_map(
        per_device, mesh=mesh, in_specs=in_specs, out_specs=out_specs, check_vma=False
    )
```

profile of v0, /device:TPU:0, one launch (start us, length us, event | category | flops | bytes accessed | tf_op | source)
XLA Modules:
  0.0 102.8 jit_solution(12264209918332326410)
XLA Ops:
  0.0 0.9 compare_reduce_fusion
  0.9 0.9 fusion.21
  1.8 0.6 copy-done.11
  2.4 0.6 dynamic-slice.4
  3.7 0.6 copy-done.10
  4.3 0.2 dynamic-update-slice
  4.5 13.1 %all-reduce = s32[16]{0:T(128)S(1)} all-reduce(s32[16]{0:T(128)S(1)} %dynamic-update-slice), channel_id=1, replica_groups=mesh['ctx'=4,'row'=8] {'row'}, use_global_device_ids=true, to_apply=%add | all-reduce | flops 16 | bytes 128
  17.6 30.8 %all_gather.25 = bf16[16,2,4096]{2,1,0:T(2,128)(2,1)S(1)} all-gather(bf16[2,2,4096]{2,1,0:T(2,128)(2,1)S(1)} %copy-done.4), channel_id=1, replica_groups=mesh['ctx'=4,'row'=8] {'row'}, dimensions={0}, use_global_device_ids=true | all-gather | bytes 294912 | tf_op jit(solution)/shard_map/all_gather | solution.py:107
  48.5 0.1 and.21
  48.8 0.1 add.73
  48.8 0.2 reshape.182
  49.1 0.6 gather_fusion.1
  49.7 0.4 copy-done.3
  50.0 0.6 gather_fusion
  50.6 0.2 broadcast_select_fusion
  50.8 0.1 reshape.129
  50.9 0.1 reshape.125
  51.0 0.5 fusion.31
  51.5 0.5 convert_reduce_fusion.1
  52.0 0.3 fusion.11
  52.3 0.9 copy-done.1
  53.2 0.3 reshape.127
  53.5 0.6 copy-done.8
  54.2 0.1 compare_and_fusion
  54.2 0.5 select_reduce_fusion
  54.8 0.9 convert_reduce_fusion
  55.7 0.1 copy.104
  55.8 0.1 copy.105
  55.8 0.7 reshape.185
  56.5 3.3 %all-to-all-start.1 = ((f32[8,1,128]{2,1,0:T(1,128)}), f32[8,1,128]{2,1,0:T(1,128)S(1)}, u32[]{:S(2)}, u32[]{:S(2)}) async-start(f32[8,1,128]{2,1,0:T(1,128)} %reshape.185), calls=%async_computation.1 | async-start | bytes 8192 | tf_op jit(solution)/shard_map/all_to_all | solution.py:137
  59.9 0.1 copy.98
  60.0 0.1 copy.99
  60.1 0.7 reshape.183
  60.8 0.3 reshape.130
  61.1 5.2 %all-to-all-done.1 = f32[8,1,128]{2,1,0:T(1,128)S(1)} async-done(((f32[8,1,128]{2,1,0:T(1,128)}), f32[8,1,128]{2,1,0:T(1,128)S(1)}, u32[]{:S(2)}, u32[]{:S(2)}) %all-to-all-start.1) | async-done | bytes 4128 | tf_op jit(solution)/shard_map/all_to_all | solution.py:137
  66.3 3.3 %all-to-all-start = ((f32[8,1,128]{2,1,0:T(1,128)}), f32[8,1,128]{2,1,0:T(1,128)S(1)}, u32[]{:S(2)}, u32[]{:S(2)}) async-start(f32[8,1,128]{2,1,0:T(1,128)} %reshape.183), calls=%async_computation | async-start | bytes 8192 | tf_op jit(solution)/shard_map/all_to_all | solution.py:136
  69.6 1.2 %fusion.7 = f32[16,2,4,8,128]{4,3,1,2,0:T(8,128)S(1)} fusion(f32[16,2,4,8,128]{4,3,1,2,0:T(8,128)S(1)} %copy.183, s32[]{:T(128)S(6)} %select_n.36, bf16[1024,4,128,1,1]{2,1,0,4,3:T(4,128)(2,1)S(1)} %bitcast.92, bf16[2,2,4,8,1024]{4,3,1,0,2:T(8,128)(2,1)} %get-tuple-element.77, f32[16,4,128,2,8]{2,4,3,1,0:T(8,128)S(1)} %fusion.11, ...), kind=kOutput, calls=%fused_computation.18 | convolution fusion | flops 33603584 | bytes 1458180 | tf_op jit(solution)/shard_map/rskgt,tkd->rskgd/dot_general | solution.py:47
  70.8 0.9 copy.179
  71.7 4.4 %all-to-all-done = f32[8,1,128]{2,1,0:T(1,128)S(1)} async-done(((f32[8,1,128]{2,1,0:T(1,128)}), f32[8,1,128]{2,1,0:T(1,128)S(1)}, u32[]{:S(2)}, u32[]{:S(2)}) %all-to-all-start) | async-done | bytes 4128 | tf_op jit(solution)/shard_map/all_to_all | solution.py:136
  76.1 3.6 %all-to-all-start.2 = ((f32[1,16,2,32,128]{4,3,2,0,1:T(8,128)}), f32[1,16,2,32,128]{4,3,2,0,1:T(8,128)S(1)}, u32[]{:S(2)}, u32[]{:S(2)}) async-start(f32[1,16,2,32,128]{4,3,2,0,1:T(8,128)} %bitcast.84), calls=%async_computation.2 | async-start | bytes 1048576 | tf_op jit(solution)/shard_map/all_to_all | solution.py:138
  79.8 0.3 select_reduce_fusion.1
  80.0 0.1 reshape.132
  80.1 0.1 convert_reduce_fusion.2
  80.3 0.1 reshape.135
  80.3 0.6 copy-done.7
  80.9 0.2 convolution_bitcast_fusion
  81.1 0.5 broadcast.101
  81.6 0.7 reduce.1
  82.3 0.1 reshape.186
  82.4 0.7 reduce
  83.1 0.1 reshape.184
  83.2 5.2 %all-gather.1 = f32[8,2,32]{2,1,0:T(2,128)S(1)} all-gather(f32[2,2,32]{2,1,0:T(2,128)S(1)} %copy.107), channel_id=3, replica_groups=mesh['ctx'=4,'row'=8] {'ctx'}, dimensions={0}, use_global_device_ids=true | all-gather | bytes 2560 | tf_op jit(solution)/shard_map/all_gather | solution.py:14
  88.4 0.6 copy-done.5
  89.0 5.1 %all-gather = f32[8,2,32]{2,1,0:T(2,128)S(1)} all-gather(f32[2,2,32]{2,1,0:T(2,128)S(1)} %copy.101), channel_id=2, replica_groups=mesh['ctx'=4,'row'=8] {'ctx'}, dimensions={0}, use_global_device_ids=true | all-gather | bytes 2560 | tf_op jit(solution)/shard_map/all_gather | solution.py:14
  94.1 0.6 copy-done.6
  94.8 0.2 multiply_reduce_fusion
  95.0 5.8 %all-gather.2 = f32[8,2,32,128]{3,2,1,0:T(8,128)S(1)} all-gather(f32[2,2,32,128]{3,2,1,0:T(8,128)S(1)} %multiply_reduce_fusion), channel_id=4, replica_groups=mesh['ctx'=4,'row'=8] {'ctx'}, dimensions={0}, use_global_device_ids=true | all-gather | bytes 327680 | tf_op jit(solution)/shard_map/all_gather | solution.py:14
  100.8 0.7 slice-done
  101.5 0.5 while.14
  101.5 0.1 fusion.36
  101.7 0.1 fusion.36
  101.9 0.1 fusion.36
  102.0 0.1 fusion.18
  102.1 0.6 reshape.136
  (51 shorter events, 0.6 us)
Async XLA Ops:
  0.0 49.0 %copy-start = (bf16[8,32,512]{2,1,0:T(8,128)(2,1)S(1)}, bf16[8,32,512]{2,1,0:T(8,128)(2,1)}, u32[]{:S(2)}) copy-start(bf16[8,32,512]{2,1,0:T(8,128)(2,1)} %param.17) | copy-start | bytes 786436
  0.0 17.6 %copy-start.4 = (bf16[2,2,4096]{2,1,0:T(2,128)(2,1)S(1)}, bf16[2,2,4096]{2,1,0:T(2,128)(2,1)}, u32[]{:S(2)}) copy-start(bf16[2,2,4096]{2,1,0:T(2,128)(2,1)} %param.14) | copy-start | bytes 98308
  1.8 0.7 copy-start.11
  3.7 0.7 copy-start.10
  49.1 1.0 copy-start.3
  52.0 1.2 %copy-start.1 = (bf16[16,64,512]{2,1,0:T(8,128)(2,1)S(1)}, bf16[16,64,512]{2,1,0:T(8,128)(2,1)}, u32[]{:S(2)}) copy-start(bf16[16,64,512]{2,1,0:T(8,128)(2,1)} %param.18) | copy-start | bytes 3145732
  53.5 0.7 copy-start.8
  54.8 6.0 %copy-start.2 = (bf16[16,64,512]{2,1,0:T(8,128)(2,1)S(1)}, bf16[16,64,512]{2,1,0:T(8,128)(2,1)}, u32[]{:S(2)}) copy-start(bf16[16,64,512]{2,1,0:T(8,128)(2,1)} %param.19) | copy-start | bytes 3145732
  56.5 9.7 %all-to-all-start.1 = ((f32[8,1,128]{2,1,0:T(1,128)}), f32[8,1,128]{2,1,0:T(1,128)S(1)}, u32[]{:S(2)}, u32[]{:S(2)}) async-start(f32[8,1,128]{2,1,0:T(1,128)} %reshape.185), calls=%async_computation.1 | async-start | bytes 8192 | tf_op jit(solution)/shard_map/all_to_all | solution.py:137
  66.3 9.8 %all-to-all-start = ((f32[8,1,128]{2,1,0:T(1,128)}), f32[8,1,128]{2,1,0:T(1,128)S(1)}, u32[]{:S(2)}, u32[]{:S(2)}) async-start(f32[8,1,128]{2,1,0:T(1,128)} %reshape.183), calls=%async_computation | async-start | bytes 8192 | tf_op jit(solution)/shard_map/all_to_all | solution.py:136
  76.1 3.6 %copy-start.9 = (bf16[2,2,512]{2,1,0:T(2,128)(2,1)S(1)}, bf16[2,2,512]{2,1,0:T(2,128)(2,1)}, u32[]{:S(2)}) copy-start(bf16[2,2,512]{2,1,0:T(2,128)(2,1)} %param.22) | copy-start | bytes 12292
  76.1 18.7 %all-to-all-start.2 = ((f32[1,16,2,32,128]{4,3,2,0,1:T(8,128)}), f32[1,16,2,32,128]{4,3,2,0,1:T(8,128)S(1)}, u32[]{:S(2)}, u32[]{:S(2)}) async-start(f32[1,16,2,32,128]{4,3,2,0,1:T(8,128)} %bitcast.84), calls=%async_computation.2 | async-start | bytes 1048576 | tf_op jit(solution)/shard_map/all_to_all | solution.py:138
  80.2 0.7 copy-start.7
  88.4 0.6 copy-start.5
  94.1 0.6 copy-start.6
  100.8 0.7 slice-start
  100.8 0.7 slice-start.1
where the time goes:
time: 103 us
  blocking collectives  60 us (58%)
  local copies, waits for them, and re-layouts  13.1 us (13%)
  starting transfers between devices  10.3 us (10%)
  waiting for transfers between devices  9.62 us (9%)
  other arithmetic  5.62 us (5%)
  matrix products  3.1 us (3%)
    all_gather x1, blocking collectives, per_device(): lax.all_gather(queries, 'row', axis=0, tiled=True)  30.8 us
    all_gather x3, blocking collectives, joined(): pieces = jax.tree.map(lambda part: lax.all_gather(part, axis), value)  16.1 us
    unnamed x1, blocking collectives  13.1 us
    unnamed x32, local copies, waits for them, and re-layouts  7.34 us
    all_to_all x1, waiting for transfers between devices, per_device(): lax.all_to_all(block_total[None], 'row', split_axis=1, concat_axis=0, til...  5.21 us
    all_to_all x1, waiting for transfers between devices, per_device(): lax.all_to_all(block_peak[None], 'row', split_axis=1, concat_axis=0, tile...  4.41 us
    all_to_all x1, starting transfers between devices, per_device(): lax.all_to_all(block_sum[None], 'row', split_axis=1, concat_axis=0, tiled...  3.62 us
    all_to_all x1, starting transfers between devices, per_device(): lax.all_to_all(block_total[None], 'row', split_axis=1, concat_axis=0, til...  3.32 us
  transfers between devices with their start and end apart: 3, of which 2 were waited for; matrix products, arithmetic and copies ran while one was open for 6% of the time, Pallas kernels for 0%

commit v1 on v0

--- a/solution.py
+++ b/solution.py
@@ -3,11 +3,33 @@
 import jax.numpy as jnp
 from jax import lax
 from jax.sharding import PartitionSpec as P
+from jax.lax import axis_index, axis_size, ppermute
 
 H = 32
 KVH = 4
 HD = 128
 MASKED_SCORE = -1e30
+
+
+def press_the_numbers(z):
+    high, lower, d_next = (axis_size("row"), axis_index("row"), z.shape[0])
+    gallery = [(d, (d + 1) % high) for d in range(high)]
+    steps_seen = [(d, (d - 1) % high) for d in range(high)]
+    r_now = jnp.zeros((*z.shape[:0], high * d_next, *z.shape[1:]), z.dtype)
+    r_now = lax.dynamic_update_slice_in_dim(r_now, z, lower * d_next, axis=0)
+    state_now = a_next = z
+    found_now = high // 2
+    for t in [*range(1, found_now + 1)]:
+        state_now = ppermute(state_now, axis_name="row", perm=gallery)
+        r_now = lax.dynamic_update_slice_in_dim(
+            r_now, state_now, (lower - t) % high * d_next, axis=0
+        )
+        if t < high - found_now:
+            a_next = ppermute(a_next, axis_name="row", perm=steps_seen)
+            r_now = lax.dynamic_update_slice_in_dim(
+                r_now, a_next, (lower + t) % high * d_next, axis=0
+            )
+    return r_now
 
 
 def joined(value, axis, join):
@@ -104,7 +126,7 @@
     causal = causal.reshape(1, step_count, 1, 1, step_count)
     fresh_stats = heads_merged(block_stats(fresh_scores, causal, fresh_values, "rskgt,rtkd->rskgd"))
     every_query, every_prefix = (
-        lax.all_gather(queries, "row", axis=0, tiled=True),
+        press_the_numbers(queries),
         lax.all_gather(prefix_id, "row", axis=0, tiled=True),
     )
     total_rows = every_query.shape[0]

time: 103 us -> 97.1 us (0.943)
  blocking collectives: 60 us -> 26.1 us
  starting transfers between devices: 10.3 us -> 25.8 us
  waiting for transfers between devices: 9.62 us -> 17.1 us
  local copies, waits for them, and re-layouts: 13.1 us -> 18.8 us
    all_gather x1 -> x0, blocking collectives: 30.8 us -> none  [per_device(): lax.all_gather(queries, 'row', axis=0, tiled=True)]
    ppermute x0 -> x7, starting transfers between devices: none -> 15.5 us  [the longest x3 12 us: press_the_numbers(): a_next = ppermute(a_next, axis_name='row', perm=steps_seen)]
    ppermute x0 -> x7, waiting for transfers between devices: none -> 6.57 us  [the longest x4 6.57 us: press_the_numbers(): state_now = ppermute(state_now, axis_name='row', perm=gallery)]
    dynamic_update_slice x0 -> x8, local copies, waits for them, and re-layouts: none -> 5.2 us  [the longest x4 2.57 us: press_the_numbers(): lax.dynamic_update_slice_in_dim(r_now, state_now, (lower - t) % high * d_...]
    unnamed x1, blocking collectives: 13.1 us -> 9.94 us
    unnamed x32 -> x35, local copies, waits for them, and re-layouts: 7.34 us -> 7.21 us
  transfers between devices with their start and end apart: 3 -> 10, of which waited for: 2 -> 5; matrix products, arithmetic and copies ran while one was open for 6% -> 17% of each run, Pallas kernels for 0% -> 0%
where the time goes in v1:
time: 97.1 us; the launch traced here: 96.5 us
  blocking collectives  26.1 us (27%)
  starting transfers between devices  25.8 us (27%)
  local copies, waits for them, and re-layouts  18.8 us (19%)
  waiting for transfers between devices  17.1 us (18%)
  other arithmetic  5.46 us (6%)
  matrix products  2.15 us (2%)
  between operations  1.18 us (1%)
    all_gather x3, blocking collectives, joined(): pieces = jax.tree.map(lambda part: lax.all_gather(part, axis), value)  16.1 us
    ppermute x3, starting transfers between devices, press_the_numbers(): a_next = ppermute(a_next, axis_name='row', perm=steps_seen)  12 us
    unnamed x1, blocking collectives  9.94 us
    unnamed x35, local copies, waits for them, and re-layouts  7.21 us
    ppermute x4, waiting for transfers between devices, press_the_numbers(): state_now = ppermute(state_now, axis_name='row', perm=gallery)  6.57 us
    all_to_all x1, waiting for transfers between devices, per_device(): lax.all_to_all(block_peak[None], 'row', split_axis=1, concat_axis=0, tile...  5.29 us
    all_to_all x1, waiting for transfers between devices, per_device(): lax.all_to_all(block_total[None], 'row', split_axis=1, concat_axis=0, til...  5.19 us
    all_to_all x1, starting transfers between devices, per_device(): lax.all_to_all(block_sum[None], 'row', split_axis=1, concat_axis=0, tiled...  3.62 us
  transfers between devices with their start and end apart: 10, of which 5 were waited for; matrix products, arithmetic and copies ran while one was open for 17% of the time, Pallas kernels for 0%

profile of v1, /device:TPU:0, one launch (start us, length us, event | category | flops | bytes accessed | tf_op | source)
XLA Modules:
  0.0 96.5 jit_solution(8057482039200172058)
XLA Ops:
  0.0 2.9 %collective-permute-start = (bf16[2,2,4096]{2,1,0:T(2,128)(2,1)}, bf16[2,2,4096]{2,1,0:T(2,128)(2,1)S(1)}, u32[]{:S(2)}, u32[]{:S(2)}) collective-permute-start(bf16[2,2,4096]{2,1,0:T(2,128)(2,1)} %param.14), channel_id=1, source_target_pairs={{0,1},{1,2},{2,3},{3,4},{4,5},{5,6},{6,7},{7,0},{8,9},{9,10},{10,1... | collective-permute-start | bytes 98312 | tf_op jit(solution)/shard_map/ppermute | solution.py:23
  2.9 3.1 %collective-permute-start.1 = (bf16[2,2,4096]{2,1,0:T(2,128)(2,1)}, bf16[2,2,4096]{2,1,0:T(2,128)(2,1)S(1)}, u32[]{:S(2)}, u32[]{:S(2)}) collective-permute-start(bf16[2,2,4096]{2,1,0:T(2,128)(2,1)} %param.14), channel_id=1, source_target_pairs={{0,7},{1,0},{2,1},{3,2},{4,3},{5,4},{6,5},{7,6},{8,15},{9,8},{10,9... | collective-permute-start | bytes 98312 | tf_op jit(solution)/shard_map/ppermute | solution.py:28
  6.0 0.9 compare_reduce_fusion
  6.9 0.9 fusion.21
  7.8 0.6 copy-done.12
  8.4 0.6 dynamic-slice.4
  9.7 0.6 copy-done.11
  10.3 0.2 dynamic-update-slice
  10.5 9.9 %all-reduce = s32[16]{0:T(128)S(1)} all-reduce(s32[16]{0:T(128)S(1)} %dynamic-update-slice), channel_id=1, replica_groups=mesh['ctx'=4,'row'=8] {'row'}, use_global_device_ids=true, to_apply=%add | all-reduce | flops 16 | bytes 128
  20.5 0.5 compare_and_fusion.1
  21.5 0.6 gather_fusion.1
  22.0 0.3 copy-done.3
  22.3 0.6 gather_fusion
  22.9 0.3 reshape.127
  23.2 0.7 broadcast_in_dim.96
  23.9 0.7 copy_dynamic-update-slice_fusion.7
  24.6 0.2 broadcast_select_fusion
  24.7 0.5 copy-done.9
  25.3 0.5 select_reduce_fusion
  25.9 0.3 convert_reduce_fusion
  26.2 0.1 reshape.129
  26.4 0.1 reshape.125
  26.5 0.6 collective-permute-start.2
  27.2 4.1 %collective-permute-start.3 = (bf16[2,2,4096]{2,1,0:T(2,128)(2,1)S(1)}, bf16[2,2,4096]{2,1,0:T(2,128)(2,1)S(1)}, u32[]{:S(2)}, u32[]{:S(2)}) collective-permute-start(bf16[2,2,4096]{2,1,0:T(2,128)(2,1)S(1)} %collective-permute-done.1), channel_id=1, source_target_pairs={{0,7},{1,0},{2,1},{3,2},{4,3},{5,4},{6,5},{7,6},{8,15},{9,8},{10,9... | collective-permute-start | bytes 98312 | tf_op jit(solution)/shard_map/ppermute | solution.py:28
  31.3 0.6 copy_dynamic-update-slice_fusion.6
  31.9 0.6 copy_dynamic-update-slice_fusion.5
  32.6 0.6 collective-permute-done.2
  33.2 4.7 %collective-permute-start.5 = (bf16[2,2,4096]{2,1,0:T(2,128)(2,1)S(1)}, bf16[2,2,4096]{2,1,0:T(2,128)(2,1)S(1)}, u32[]{:S(2)}, u32[]{:S(2)}) collective-permute-start(bf16[2,2,4096]{2,1,0:T(2,128)(2,1)S(1)} %collective-permute-done.3), channel_id=1, source_target_pairs={{0,7},{1,0},{2,1},{3,2},{4,3},{5,4},{6,5},{7,6},{8,15},{9,8},{10,9... | collective-permute-start | bytes 98312 | tf_op jit(solution)/shard_map/ppermute | solution.py:28
  37.9 0.6 copy_dynamic-update-slice_fusion.4
  38.6 0.7 copy_dynamic-update-slice_fusion.3
  39.2 0.7 collective-permute-done.4
  39.9 0.7 copy_dynamic-update-slice_fusion.2
  40.6 0.7 copy_dynamic-update-slice_fusion.1
  41.2 5.3 %collective-permute-done.6 = bf16[2,2,4096]{2,1,0:T(2,128)(2,1)S(1)} collective-permute-done((bf16[2,2,4096]{2,1,0:T(2,128)(2,1)S(1)}, bf16[2,2,4096]{2,1,0:T(2,128)(2,1)S(1)}, u32[]{:S(2)}, u32[]{:S(2)}) %collective-permute-start.6) | collective-permute-done | bytes 32800 | tf_op jit(solution)/shard_map/ppermute | solution.py:23
  46.5 0.6 copy_dynamic-update-slice_fusion
  47.2 1.0 %copy.162 = bf16[4,8,32,128]{3,2,1,0:T(8,128)(2,1)S(1)} copy(bf16[4,8,32,128]{3,1,2,0:T(8,128)(2,1)} %bitcast.39) | data formatting | bytes 524288
  48.1 0.5 fusion.31
  48.7 0.5 convert_reduce_fusion.1
  49.1 0.3 fusion.11
  49.7 0.7 reshape.184
  50.4 3.3 %all-to-all-start.1 = ((f32[8,1,128]{2,1,0:T(1,128)}), f32[8,1,128]{2,1,0:T(1,128)S(1)}, u32[]{:S(2)}, u32[]{:S(2)}) async-start(f32[8,1,128]{2,1,0:T(1,128)} %reshape.184), calls=%async_computation.1 | async-start | bytes 8192 | tf_op jit(solution)/shard_map/all_to_all | solution.py:159
  53.7 0.3 reshape.130
  54.2 0.7 reshape.182
  54.9 5.2 %all-to-all-done.1 = f32[8,1,128]{2,1,0:T(1,128)S(1)} async-done(((f32[8,1,128]{2,1,0:T(1,128)}), f32[8,1,128]{2,1,0:T(1,128)S(1)}, u32[]{:S(2)}, u32[]{:S(2)}) %all-to-all-start.1) | async-done | bytes 4128 | tf_op jit(solution)/shard_map/all_to_all | solution.py:159
  60.1 3.3 %all-to-all-start = ((f32[8,1,128]{2,1,0:T(1,128)}), f32[8,1,128]{2,1,0:T(1,128)S(1)}, u32[]{:S(2)}, u32[]{:S(2)}) async-start(f32[8,1,128]{2,1,0:T(1,128)} %reshape.182), calls=%async_computation | async-start | bytes 8192 | tf_op jit(solution)/shard_map/all_to_all | solution.py:158
  63.4 0.3 fusion.7
  63.7 0.9 copy.214
  64.6 5.3 %all-to-all-done = f32[8,1,128]{2,1,0:T(1,128)S(1)} async-done(((f32[8,1,128]{2,1,0:T(1,128)}), f32[8,1,128]{2,1,0:T(1,128)S(1)}, u32[]{:S(2)}, u32[]{:S(2)}) %all-to-all-start) | async-done | bytes 4128 | tf_op jit(solution)/shard_map/all_to_all | solution.py:158
  69.9 3.6 %all-to-all-start.2 = ((f32[1,16,2,32,128]{4,3,2,0,1:T(8,128)}), f32[1,16,2,32,128]{4,3,2,0,1:T(8,128)S(1)}, u32[]{:S(2)}, u32[]{:S(2)}) async-start(f32[1,16,2,32,128]{4,3,2,0,1:T(8,128)} %bitcast.90), calls=%async_computation.2 | async-start | bytes 1048576 | tf_op jit(solution)/shard_map/all_to_all | solution.py:160
  73.5 0.3 select_reduce_fusion.1
  74.1 0.6 copy-done.7
  74.7 0.2 convolution_bitcast_fusion
  74.9 0.5 broadcast.108
  75.4 0.7 reduce.1
  76.2 0.7 reduce
  77.0 5.2 %all-gather.1 = f32[8,2,32]{2,1,0:T(2,128)S(1)} all-gather(f32[2,2,32]{2,1,0:T(2,128)S(1)} %copy.135), channel_id=3, replica_groups=mesh['ctx'=4,'row'=8] {'ctx'}, dimensions={0}, use_global_device_ids=true | all-gather | bytes 2560 | tf_op jit(solution)/shard_map/all_gather | solution.py:36
  82.2 0.6 copy-done.5
  82.8 5.1 %all-gather = f32[8,2,32]{2,1,0:T(2,128)S(1)} all-gather(f32[2,2,32]{2,1,0:T(2,128)S(1)} %copy.129), channel_id=2, replica_groups=mesh['ctx'=4,'row'=8] {'ctx'}, dimensions={0}, use_global_device_ids=true | all-gather | bytes 2560 | tf_op jit(solution)/shard_map/all_gather | solution.py:36
  87.9 0.6 copy-done.6
  88.5 0.2 multiply_reduce_fusion
  88.7 5.8 %all-gather.2 = f32[8,2,32,128]{3,2,1,0:T(8,128)S(1)} all-gather(f32[2,2,32,128]{3,2,1,0:T(8,128)S(1)} %multiply_reduce_fusion), channel_id=4, replica_groups=mesh['ctx'=4,'row'=8] {'ctx'}, dimensions={0}, use_global_device_ids=true | all-gather | bytes 327680 | tf_op jit(solution)/shard_map/all_gather | solution.py:36
  94.6 0.7 slice-done
  95.3 0.5 while.14
  95.9 0.6 reshape.136
  (75 shorter events, 2.1 us)
Async XLA Ops:
  0.0 21.4 %copy-start = (bf16[8,32,512]{2,1,0:T(8,128)(2,1)S(1)}, bf16[8,32,512]{2,1,0:T(8,128)(2,1)}, u32[]{:S(2)}) copy-start(bf16[8,32,512]{2,1,0:T(8,128)(2,1)} %param.17) | copy-start | bytes 786436
  0.0 21.0 %copy-start.4 = (bf16[2,2,4096]{2,1,0:T(2,128)(2,1)S(1)}, bf16[2,2,4096]{2,1,0:T(2,128)(2,1)}, u32[]{:S(2)}) copy-start(bf16[2,2,4096]{2,1,0:T(2,128)(2,1)} %param.14) | copy-start | bytes 98308
  0.0 26.5 %collective-permute-start = (bf16[2,2,4096]{2,1,0:T(2,128)(2,1)}, bf16[2,2,4096]{2,1,0:T(2,128)(2,1)S(1)}, u32[]{:S(2)}, u32[]{:S(2)}) collective-permute-start(bf16[2,2,4096]{2,1,0:T(2,128)(2,1)} %param.14), channel_id=1, source_target_pairs={{0,1},{1,2},{2,3},{3,4},{4,5},{5,6},{6,7},{7,0},{8,9},{9,10},{10,1... | collective-permute-start | bytes 98312 | tf_op jit(solution)/shard_map/ppermute | solution.py:23
  2.9 24.2 %collective-permute-start.1 = (bf16[2,2,4096]{2,1,0:T(2,128)(2,1)}, bf16[2,2,4096]{2,1,0:T(2,128)(2,1)S(1)}, u32[]{:S(2)}, u32[]{:S(2)}) collective-permute-start(bf16[2,2,4096]{2,1,0:T(2,128)(2,1)} %param.14), channel_id=1, source_target_pairs={{0,7},{1,0},{2,1},{3,2},{4,3},{5,4},{6,5},{7,6},{8,15},{9,8},{10,9... | collective-permute-start | bytes 98312 | tf_op jit(solution)/shard_map/ppermute | solution.py:28
  7.8 0.7 copy-start.12
  9.7 0.7 copy-start.11
  21.3 1.0 copy-start.3
  21.4 1.5 %copy-start.1 = (bf16[16,64,512]{2,1,0:T(8,128)(2,1)S(1)}, bf16[16,64,512]{2,1,0:T(8,128)(2,1)}, u32[]{:S(2)}) copy-start(bf16[16,64,512]{2,1,0:T(8,128)(2,1)} %param.18) | copy-start | bytes 3145732
  23.9 0.7 copy-start.8
  24.6 0.7 copy-start.9
  26.5 6.7 %collective-permute-start.2 = (bf16[2,2,4096]{2,1,0:T(2,128)(2,1)S(1)}, bf16[2,2,4096]{2,1,0:T(2,128)(2,1)S(1)}, u32[]{:S(2)}, u32[]{:S(2)}) collective-permute-start(bf16[2,2,4096]{2,1,0:T(2,128)(2,1)S(1)} %collective-permute-done), channel_id=1, source_target_pairs={{0,1},{1,2},{2,3},{3,4},{4,5},{5,6},{6,7},{7,0},{8,9},{9,10},{10,1... | collective-permute-start | bytes 98312 | tf_op jit(solution)/shard_map/ppermute | solution.py:23
  27.2 6.0 %collective-permute-start.3 = (bf16[2,2,4096]{2,1,0:T(2,128)(2,1)S(1)}, bf16[2,2,4096]{2,1,0:T(2,128)(2,1)S(1)}, u32[]{:S(2)}, u32[]{:S(2)}) collective-permute-start(bf16[2,2,4096]{2,1,0:T(2,128)(2,1)S(1)} %collective-permute-done.1), channel_id=1, source_target_pairs={{0,7},{1,0},{2,1},{3,2},{4,3},{5,4},{6,5},{7,6},{8,15},{9,8},{10,9... | collective-permute-start | bytes 98312 | tf_op jit(solution)/shard_map/ppermute | solution.py:28
  33.2 6.7 %collective-permute-start.4 = (bf16[2,2,4096]{2,1,0:T(2,128)(2,1)S(1)}, bf16[2,2,4096]{2,1,0:T(2,128)(2,1)S(1)}, u32[]{:S(2)}, u32[]{:S(2)}) collective-permute-start(bf16[2,2,4096]{2,1,0:T(2,128)(2,1)S(1)} %collective-permute-done.2), channel_id=1, source_target_pairs={{0,1},{1,2},{2,3},{3,4},{4,5},{5,6},{6,7},{7,0},{8,9},{9,10},{10,1... | collective-permute-start | bytes 98312 | tf_op jit(solution)/shard_map/ppermute | solution.py:23
  33.2 7.4 %collective-permute-start.5 = (bf16[2,2,4096]{2,1,0:T(2,128)(2,1)S(1)}, bf16[2,2,4096]{2,1,0:T(2,128)(2,1)S(1)}, u32[]{:S(2)}, u32[]{:S(2)}) collective-permute-start(bf16[2,2,4096]{2,1,0:T(2,128)(2,1)S(1)} %collective-permute-done.3), channel_id=1, source_target_pairs={{0,7},{1,0},{2,1},{3,2},{4,3},{5,4},{6,5},{7,6},{8,15},{9,8},{10,9... | collective-permute-start | bytes 98312 | tf_op jit(solution)/shard_map/ppermute | solution.py:28
  39.9 6.6 %collective-permute-start.6 = (bf16[2,2,4096]{2,1,0:T(2,128)(2,1)S(1)}, bf16[2,2,4096]{2,1,0:T(2,128)(2,1)S(1)}, u32[]{:S(2)}, u32[]{:S(2)}) collective-permute-start(bf16[2,2,4096]{2,1,0:T(2,128)(2,1)S(1)} %collective-permute-done.4), channel_id=1, source_target_pairs={{0,1},{1,2},{2,3},{3,4},{4,5},{5,6},{6,7},{7,0},{8,9},{9,10},{10,1... | collective-permute-start | bytes 98312 | tf_op jit(solution)/shard_map/ppermute | solution.py:23
  49.1 4.6 %copy-start.2 = (bf16[16,64,512]{2,1,0:T(8,128)(2,1)S(1)}, bf16[16,64,512]{2,1,0:T(8,128)(2,1)}, u32[]{:S(2)}) copy-start(bf16[16,64,512]{2,1,0:T(8,128)(2,1)} %param.19) | copy-start | bytes 3145732
  50.4 9.7 %all-to-all-start.1 = ((f32[8,1,128]{2,1,0:T(1,128)}), f32[8,1,128]{2,1,0:T(1,128)S(1)}, u32[]{:S(2)}, u32[]{:S(2)}) async-start(f32[8,1,128]{2,1,0:T(1,128)} %reshape.184), calls=%async_computation.1 | async-start | bytes 8192 | tf_op jit(solution)/shard_map/all_to_all | solution.py:159
  60.1 9.8 %all-to-all-start = ((f32[8,1,128]{2,1,0:T(1,128)}), f32[8,1,128]{2,1,0:T(1,128)S(1)}, u32[]{:S(2)}, u32[]{:S(2)}) async-start(f32[8,1,128]{2,1,0:T(1,128)} %reshape.182), calls=%async_computation | async-start | bytes 8192 | tf_op jit(solution)/shard_map/all_to_all | solution.py:158
  69.9 3.6 %copy-start.10 = (bf16[2,2,512]{2,1,0:T(2,128)(2,1)S(1)}, bf16[2,2,512]{2,1,0:T(2,128)(2,1)}, u32[]{:S(2)}) copy-start(bf16[2,2,512]{2,1,0:T(2,128)(2,1)} %param.22) | copy-start | bytes 12292
  69.9 18.7 %all-to-all-start.2 = ((f32[1,16,2,32,128]{4,3,2,0,1:T(8,128)}), f32[1,16,2,32,128]{4,3,2,0,1:T(8,128)S(1)}, u32[]{:S(2)}, u32[]{:S(2)}) async-start(f32[1,16,2,32,128]{4,3,2,0,1:T(8,128)} %bitcast.90), calls=%async_computation.2 | async-start | bytes 1048576 | tf_op jit(solution)/shard_map/all_to_all | solution.py:160
  74.0 0.7 copy-start.7
  82.2 0.6 copy-start.5
  87.9 0.6 copy-start.6
  94.6 0.7 slice-start
  94.6 0.7 slice-start.1
